TPU v7x, 256 devices: a whole 4x4x8 slice. The times are simulated.
256 devices in a mesh: blocks: 64 (over z, x, core), chan: 4 (over y).
Axes of the slice: x: 4, y: 4, z: 8, core: 2. Of those that a mesh axis runs over, the one named last changes fastest.
Arguments:
- fine_input: bfloat16 [1024, 64, 512], P('blocks', 'chan'), may hold values from -6 to 6
- block_counts: int32 [64], replicated, may hold values from 8 to 16, as said below
- fine_weight: bfloat16 [7, 64, 64], P(None, 'chan'), may hold values from -0.25 to 0.25
- fine_bias: float32 [64], P('chan'), may hold values from -3 to 3
- coarse_weight: bfloat16 [7, 64, 64], P(None, 'chan'), may hold values from -0.25 to 0.25
- coarse_bias: float32 [64], P('chan'), may hold values from -3 to 3
- coarse_cotangent: bfloat16 [128, 64, 512], P('blocks', 'chan'), may hold values from -48 to 48
Outputs:
- coarser_level_output: bfloat16 [128, 64, 512], P('blocks', 'chan')
- fine_grad: bfloat16 [1024, 64, 512], P('blocks', 'chan')
- fine_weight_grad: float32 [7, 64, 64], P(None, 'chan')
- fine_bias_grad: float32 [64], P('chan')
- coarse_weight_grad: float32 [7, 64, 64], P(None, 'chan')
- coarse_bias_grad: float32 [64], P('chan')
Inputs may be any that keep to these rules, and one draw needn't show every extreme that they name: `block_counts`: fine blocks held by each device of blocks; they sum to 768, and some device holds exactly 16.
All inputs are finite; a program needn't handle non-finite values.
Results may differ from a plain program's by a relative error of at most 0.017.
Values may be sent and summed in bfloat16 or wider, within the bound.
No kernel may reach another device: no remote copies, remote signals or barrier semaphores. Data moves between devices by JAX's collectives and lax.ppermute only.
A program may use at most 64 MiB of HBM per device.

v0:
```python
import jax
import jax.numpy as jnp
from jax import lax
from jax.sharding import PartitionSpec as P

EDGE = 8
TAP_PAIRS = (0, 2, 1, 4, 3, 6, 5)


def from_behind(block, axis, distance):
    devices = range(lax.axis_size(axis))
    route = [(i - distance, i) for i in devices if i - distance in devices]
    return lax.ppermute(block, axis, route)


def block_layers(block_cube):
    channels, edge_cells = (block_cube.shape[0], block_cube.shape[1])
    side_layers = [
        block_cube[:, :, :, 0],
        block_cube[:, :, :, -1],
        block_cube[:, :, 0, :],
        block_cube[:, :, -1, :],
        block_cube[:, 0],
        block_cube[:, -1],
    ]
    return jnp.stack(side_layers).reshape(6, channels, edge_cells * edge_cells)


def block_views(block_cube, halo_layers):
    channels, edge_cells = (block_cube.shape[0], block_cube.shape[1])
    sheets = halo_layers.reshape(6, channels, edge_cells, edge_cells)
    minus_x = jnp.concatenate([sheets[0][:, :, :, None], block_cube[:, :, :, :-1]], axis=3)
    plus_x = jnp.concatenate([block_cube[:, :, :, 1:], sheets[1][:, :, :, None]], axis=3)
    minus_y = jnp.concatenate([sheets[2][:, :, None, :], block_cube[:, :, :-1, :]], axis=2)
    plus_y = jnp.concatenate([block_cube[:, :, 1:, :], sheets[3][:, :, None, :]], axis=2)
    minus_z = jnp.concatenate([sheets[4][:, None], block_cube[:, :-1]], axis=1)
    plus_z = jnp.concatenate([block_cube[:, 1:], sheets[5][:, None]], axis=1)
    stacked = jnp.stack([block_cube, minus_x, plus_x, minus_y, plus_y, minus_z, plus_z])
    return stacked.reshape(7 * channels, edge_cells**3)


def slope_of(pre_values):
    sigmoid_values = jax.nn.sigmoid(pre_values)
    return sigmoid_values * (1.0 + pre_values * (1.0 - sigmoid_values))


def fine_halo(layer_table, block_ids, first_block, live_count, total_blocks):
    slot_count = layer_table.shape[0]
    plus_side = layer_table[:, 1::2]
    minus_side = layer_table[:, 0::2]
    tail_layers = lax.dynamic_slice_in_dim(plus_side, live_count - 4, 4, 0)
    from_lower = from_behind(tail_layers, "blocks", 1)
    from_upper = from_behind(minus_side[:4], "blocks", -1)
    table_minus = jnp.concatenate([from_lower, plus_side], axis=0)
    table_plus = jnp.concatenate([minus_side, from_upper], axis=0)
    strides = jnp.array([1, 2, 4], jnp.int32)
    lower_ids = block_ids[:, None] - strides[None, :]
    upper_octant_index = block_ids[:, None] + strides[None, :]
    end_block = first_block + live_count
    rows_minus = jnp.clip(lower_ids - first_block + 4, 0, slot_count + 3)
    rows_plus = jnp.clip(
        jnp.where(
            upper_octant_index < end_block,
            upper_octant_index - first_block,
            slot_count + upper_octant_index - end_block,
        ),
        0,
        slot_count + 3,
    )
    columns = jnp.arange(3, dtype=jnp.int32)[None, :]
    got_minus = table_minus[rows_minus, columns]
    got_plus = table_plus[rows_plus, columns]
    parity_x = block_ids % 2
    parity_y = block_ids // 2 % 2
    keep_minus = jnp.stack([parity_x == 1, parity_y == 1, block_ids >= 4], axis=1)
    keep_plus = jnp.stack([parity_x == 0, parity_y == 0, block_ids + 4 < total_blocks], axis=1)
    zero_value = jnp.zeros((), layer_table.dtype)
    got_minus = jnp.where(keep_minus[:, :, None, None], got_minus, zero_value)
    got_plus = jnp.where(keep_plus[:, :, None, None], got_plus, zero_value)
    merged = jnp.stack([got_minus, got_plus], axis=2)
    return merged.reshape(layer_table.shape)


def coarse_halo(layer_table, coarse_ids, coarse_first, coarse_count, coarse_total):
    slot_count = layer_table.shape[0]
    top_layers = layer_table[:, 5]
    bottom_layers = layer_table[:, 4]
    last_top = lax.dynamic_index_in_dim(top_layers, coarse_count - 1, 0, keepdims=False)
    from_lower = from_behind(last_top, "blocks", 1)
    from_upper = from_behind(bottom_layers[0], "blocks", -1)
    table_minus = jnp.concatenate([from_lower[None], top_layers], axis=0)
    table_plus = jnp.concatenate([bottom_layers, from_upper[None]], axis=0)
    rows_minus = jnp.clip(coarse_ids - coarse_first, 0, slot_count)
    rows_plus = jnp.clip(
        jnp.where(
            coarse_ids + 1 < coarse_first + coarse_count, coarse_ids + 1 - coarse_first, slot_count
        ),
        0,
        slot_count,
    )
    zero_value = jnp.zeros((), layer_table.dtype)
    below_layer = jnp.where((coarse_ids >= 1)[:, None, None], table_minus[rows_minus], zero_value)
    above_layer = jnp.where(
        (coarse_ids + 1 < coarse_total)[:, None, None], table_plus[rows_plus], zero_value
    )
    flat_zero = jnp.zeros_like(below_layer)
    return jnp.stack([flat_zero, flat_zero, flat_zero, flat_zero, below_layer, above_layer], axis=1)


def apply_blocks(matrix, block_cubes, halo_table):

    def one_block(operands):
        return jnp.dot(
            matrix, block_views(operands[0], operands[1]), preferred_element_type=jnp.float32
        )

    return lax.map(one_block, (block_cubes, halo_table))


def weight_block(operands):
    tap_views = block_views(operands[0], operands[1])
    return lax.dot_general(
        operands[2], tap_views, (((1,), (1,)), ((), ())), preferred_element_type=jnp.float32
    )


def restrict_blocks(hidden, half_edge):
    count, width = (hidden.shape[0], hidden.shape[1])
    shaped = hidden.reshape(count, width, half_edge, 2, half_edge, 2, half_edge, 2)
    return (
        (jnp.sum(shaped, axis=(3, 5, 7), dtype=jnp.float32) * 0.125)
        .astype(jnp.bfloat16)
        .reshape(count, width, half_edge**3)
    )


def sum_over_blocks(parts):
    chan_index = lax.axis_index("chan")
    chan_count = lax.axis_size("chan")
    flat = jnp.concatenate([part.reshape(-1) for part in parts])
    slots = jnp.zeros((chan_count, flat.shape[0]), flat.dtype)
    slots = lax.dynamic_update_index_in_dim(slots, flat, chan_index, 0)
    summed = lax.psum(slots, ("blocks", "chan"))
    mine = lax.dynamic_index_in_dim(summed, chan_index, 0, keepdims=False)
    pieces = []
    offset = 0
    for part in parts:
        pieces.append(mine[offset : offset + part.size].reshape(part.shape))
        offset += part.size
    return tuple(pieces)


def local(
    fine_input, block_counts, fine_weight, fine_bias, coarse_weight, coarse_bias, coarse_cotangent
):
    slot_count, group_size, cell_count = fine_input.shape
    coarse_slots = coarse_cotangent.shape[0]
    channels = fine_weight.shape[2]
    half_edge = EDGE // 2
    octant_cells = half_edge**3
    pair_index = jnp.array(TAP_PAIRS, jnp.int32)
    device = lax.axis_index("blocks")
    starts = jnp.cumsum(block_counts) - block_counts
    first_block = starts[device]
    live_count = block_counts[device]
    end_block = first_block + live_count
    total_blocks = jnp.sum(block_counts)
    coarse_total = total_blocks // 8
    coarse_first = (first_block + 7) // 8
    coarse_count = (end_block + 7) // 8 - coarse_first
    block_ids = first_block + jnp.arange(slot_count, dtype=jnp.int32)
    coarse_ids = coarse_first + jnp.arange(coarse_slots, dtype=jnp.int32)
    live_mask = (jnp.arange(slot_count) < live_count)[:, None, None]
    coarse_live = (jnp.arange(coarse_slots) < coarse_count)[:, None, None]
    full_input = lax.all_gather(fine_input, "chan", axis=1, tiled=True)
    fine_cubes = full_input.reshape(slot_count, channels, EDGE, EDGE, EDGE)
    input_halos = fine_halo(
        jax.vmap(block_layers)(fine_cubes), block_ids, first_block, live_count, total_blocks
    )
    forward_fine = fine_weight.transpose(1, 0, 2).reshape(group_size, 7 * channels)
    fine_views = jax.vmap(block_views)(fine_cubes, input_halos)
    pre_fine = (
        jnp.einsum("ln,bnp->blp", forward_fine, fine_views, preferred_element_type=jnp.float32)
        + fine_bias[None, :, None]
    )
    octants = restrict_blocks(jax.nn.silu(pre_fine).astype(jnp.bfloat16), half_edge)
    upper_octants = from_behind(octants[:7], "blocks", -1)
    octant_table = jnp.concatenate([octants, upper_octants], axis=0)
    children = coarse_ids[:, None] * 8 + jnp.arange(8, dtype=jnp.int32)[None, :]
    child_rows = jnp.clip(
        jnp.where(children < end_block, children - first_block, slot_count + children - end_block),
        0,
        slot_count + 6,
    )
    gathered = octant_table[child_rows]
    coarse_local = (
        gathered.reshape(coarse_slots, 2, 2, 2, group_size, half_edge, half_edge, half_edge)
        .transpose(0, 4, 1, 5, 2, 6, 3, 7)
        .reshape(coarse_slots, group_size, cell_count)
    )
    coarse_local = jnp.where(coarse_live, coarse_local, jnp.zeros((), jnp.bfloat16))
    coarse_full = lax.all_gather(coarse_local, "chan", axis=1, tiled=True)
    coarse_cubes = coarse_full.reshape(coarse_slots, channels, EDGE, EDGE, EDGE)
    coarse_in_halos = coarse_halo(
        jax.vmap(block_layers)(coarse_cubes), coarse_ids, coarse_first, coarse_count, coarse_total
    )
    coarser_level_views = jax.vmap(block_views)(coarse_cubes, coarse_in_halos)
    forward_coarser_level = coarse_weight.transpose(1, 0, 2).reshape(group_size, 7 * channels)
    pre_coarse = (
        jnp.einsum(
            "ln,enp->elp",
            forward_coarser_level,
            coarser_level_views,
            preferred_element_type=jnp.float32,
        )
        + coarse_bias[None, :, None]
    )
    coarser_level_output = jnp.where(coarse_live, jax.nn.silu(pre_coarse), 0.0).astype(jnp.bfloat16)
    coarser_level_delta = jnp.where(
        coarse_live, coarse_cotangent.astype(jnp.float32) * slope_of(pre_coarse), 0.0
    ).astype(jnp.bfloat16)
    coarse_weight_grad = jnp.einsum(
        "zlc,znc->ln", coarser_level_delta, coarser_level_views, preferred_element_type=jnp.float32
    )
    coarse_weight_grad = coarse_weight_grad.reshape(group_size, 7, channels).transpose(1, 0, 2)
    coarse_bias_grad = jnp.sum(coarser_level_delta, axis=(0, 2), dtype=jnp.float32)
    delta_cubes = coarser_level_delta.reshape(coarse_slots, group_size, EDGE, EDGE, EDGE)
    delta_halos = coarse_halo(
        jax.vmap(block_layers)(delta_cubes), coarse_ids, coarse_first, coarse_count, coarse_total
    )
    delta_window_views = jax.vmap(block_views)(delta_cubes, delta_halos)
    backward_coarser_level = (
        coarse_weight[pair_index].transpose(2, 0, 1).reshape(channels, 7 * group_size)
    )
    partial_sums = jnp.einsum(
        "ur,mre->mue",
        backward_coarser_level,
        delta_window_views,
        preferred_element_type=jnp.float32,
    )
    coarse_back = lax.psum_scatter(
        partial_sums.astype(jnp.bfloat16), "chan", scatter_dimension=1, tiled=True
    ).astype(jnp.float32)
    coarse_back = jnp.where(coarse_live, coarse_back, 0.0).astype(jnp.bfloat16)
    coarse_octants = (
        coarse_back.reshape(coarse_slots, group_size, 2, half_edge, 2, half_edge, 2, half_edge)
        .transpose(0, 2, 4, 6, 1, 3, 5, 7)
        .reshape(coarse_slots * 8, group_size, octant_cells)
    )
    last_octants = lax.dynamic_slice_in_dim(coarse_octants, (coarse_count - 1) * 8 + 1, 7, 0)
    lower_octants = from_behind(last_octants, "blocks", 1)
    back_table = jnp.concatenate([coarse_octants, lower_octants], axis=0)
    parents = block_ids // 8
    octant_ids = block_ids % 8
    back_rows = jnp.clip(
        jnp.where(
            parents >= coarse_first,
            (parents - coarse_first) * 8 + octant_ids,
            coarse_slots * 8 + octant_ids - 1,
        ),
        0,
        coarse_slots * 8 + 6,
    )
    picked_rows = back_table[back_rows]
    picked = picked_rows.reshape(slot_count, group_size, half_edge, 1, half_edge, 1, half_edge, 1)
    widened = jnp.broadcast_to(
        picked, (slot_count, group_size, half_edge, 2, half_edge, 2, half_edge, 2)
    ).reshape(slot_count, group_size, cell_count)
    fine_delta = jnp.where(
        live_mask, widened.astype(jnp.float32) * 0.125 * slope_of(pre_fine), 0.0
    ).astype(jnp.bfloat16)
    fine_weight_grad = jnp.einsum(
        "blp,bnp->ln", fine_delta, fine_views, preferred_element_type=jnp.float32
    )
    fine_weight_grad = fine_weight_grad.reshape(group_size, 7, channels).transpose(1, 0, 2)
    fine_bias_grad = jnp.sum(fine_delta, axis=(0, 2), dtype=jnp.float32)
    fine_delta_cubes = fine_delta.reshape(slot_count, group_size, EDGE, EDGE, EDGE)
    fine_delta_halos = fine_halo(
        jax.vmap(block_layers)(fine_delta_cubes), block_ids, first_block, live_count, total_blocks
    )
    back_fine = fine_weight[pair_index].transpose(2, 0, 1).reshape(channels, 7 * group_size)
    fine_delta_views = jax.vmap(block_views)(fine_delta_cubes, fine_delta_halos)
    fine_partial = jnp.einsum(
        "ur,bre->bue", back_fine, fine_delta_views, preferred_element_type=jnp.float32
    )
    fine_back = lax.psum_scatter(
        fine_partial.astype(jnp.bfloat16), "chan", scatter_dimension=1, tiled=True
    ).astype(jnp.float32)
    fine_grad = jnp.where(live_mask, fine_back, 0.0).astype(jnp.bfloat16)
    fine_weight_grad, fine_bias_grad, coarse_weight_grad, coarse_bias_grad = sum_over_blocks(
        (fine_weight_grad, fine_bias_grad, coarse_weight_grad, coarse_bias_grad)
    )
    fine_norm = jnp.sqrt(total_blocks.astype(jnp.float32) * cell_count)
    coarse_norm = jnp.sqrt(coarse_total.astype(jnp.float32) * cell_count)
    return (
        coarser_level_output,
        fine_grad,
        fine_weight_grad / fine_norm,
        fine_bias_grad / fine_norm,
        coarse_weight_grad / coarse_norm,
        coarse_bias_grad / coarse_norm,
    )


def solution(mesh):
    placed = (
        P("blocks", "chan", None),
        P(),
        P(None, "chan", None),
        P("chan"),
        P(None, "chan", None),
        P("chan"),
        P("blocks", "chan", None),
    )
    return jax.shard_map(
        local,
        mesh=mesh,
        in_specs=placed,
        out_specs=(
            P("blocks", "chan", None),
            P("blocks", "chan", None),
            P(None, "chan", None),
            P("chan"),
            P(None, "chan", None),
            P("chan"),
        ),
        check_vma=False,
    )
```

profile of v0, /device:TPU:6, one launch (start us, length us, event | category | flops | bytes accessed | tf_op | source)
XLA Modules:
  0.0 571.9 jit_solution(10096941222904606873)
XLA Ops:
  26.3 13.6 %all-gather.2.cloned.1.call-done = bf16[16,64,512]{2,0,1:T(8,128)(2,1)} async-done(((bf16[16,16,512]{2,0,1:T(8,128)(2,1)}), bf16[16,64,512]{2,0,1:T(8,128)(2,1)}) %all-gather.2.cloned.1.call-update) | async-done | bytes 1048592 | tf_op jit(solution)/shard_map/all_gather | solution.py:175
  40.0 2.4 copy.325
  43.4 2.9 fusion.73
  46.4 2.9 fusion.72
  49.3 3.0 fusion.71
  53.0 1.9 collective-permute-start
  54.9 3.6 collective-permute-start.1
  72.0 2.7 fusion.2
  74.7 2.7 fusion.3
  77.5 2.0 fusion.4
  79.4 1.9 fusion.5
  81.4 2.0 fusion.6
  83.4 1.9 fusion.7
  85.4 33.5 %copy.344 = bf16[16,7,64,8,8,8]{2,1,5,4,3,0:T(8,128)(2,1)} copy(bf16[16,7,64,8,8,8]{2,5,4,3,0,1:T(8,128)(2,1)} %bitcast.418) | data formatting | bytes 14680064 | tf_op jit(solution)/shard_map/vmap()/transpose | solution.py:39
  118.9 22.2 %reshape.836 = bf16[16,448,512]{1,2,0:T(8,128)(2,1)} reshape(bf16[16,7,64,8,8,8]{2,1,5,4,3,0:T(8,128)(2,1)} %copy.344) | data formatting | bytes 14680064 | tf_op jit(solution)/shard_map/vmap()/reshape | solution.py:39
  141.1 6.5 %fusion.21 = (f32[16,16,512]{2,1,0:T(8,128)S(1)}, f32[16,16,512]{2,1,0:T(8,128)}) fusion(f32[16]{0:T(128)S(1)} %copy-done.27, bf16[16,448,512]{1,2,0:T(8,128)(2,1)} %reshape.836, bf16[16,448,1]{1,0,2:T(8,128)(2,1)S(1)} %reshape.951), kind=kOutput, calls=%fused_computation.62 | convolution fusion | flops 118358016 | bytes 8403008 | tf_op jit(solution)/shard_map/ln,bnp->blp/dot_general | solution.py:183
  147.6 3.7 copy.347
  151.3 2.8 reduce_sum.37
  154.3 1.9 collective-permute-start.2
  160.1 12.0 %all_gather.7 = bf16[2,64,512]{2,1,0:T(8,128)(2,1)S(1)} all-gather(bf16[2,16,512]{2,1,0:T(8,128)(2,1)S(1)} %broadcast_select_fusion.4), channel_id=1, replica_groups=mesh['blocks'=64,'chan'=4] {'chan'}, dimensions={1}, use_global_device_ids=true | all-gather | bytes 163840 | tf_op jit(solution)/shard_map/all_gather | solution.py:202
  172.8 1.9 collective-permute-start.4
  174.7 3.7 collective-permute-start.3
  181.9 4.3 copy.364
  192.6 1.9 collective-permute-start.6
  195.2 5.9 %collective-permute-start.5 = (bf16[16,64]{1,0:T(8,128)(2,1)}, bf16[16,64]{1,0:T(8,128)(2,1)}, u32[]{:S(2)}, u32[]{:S(2)}) collective-permute-start(bf16[16,64]{1,0:T(8,128)(2,1)} %bitcast.86), channel_id=1, source_target_pairs={{0,4},{4,8},{8,12},{12,16},{16,20},{20,24},{24,28},{28,32},{32,36}... | collective-permute-start | bytes 6152 | tf_op jit(solution)/shard_map/ppermute | solution.py:13
  210.5 4.3 copy.383
  219.5 14.8 %copy.416 = bf16[448,16,512]{2,1,0:T(8,128)(2,1)} copy(bf16[448,16,512]{0,2,1:T(8,128)(2,1)} %bitcast.416) | data formatting | bytes 14680064 | tf_op jit(solution)/shard_map/blp,bnp->ln/dot_general | solution.py:272
  234.8 12.7 %reduce-scatter.3.cloned.1.call-done = bf16[2,16,512]{2,1,0:T(8,128)(2,1)} async-done(((bf16[2,64,512]{2,1,0:T(8,128)(2,1)}), bf16[2,16,512]{2,1,0:T(8,128)(2,1)}) %reduce-scatter.3.cloned.1.call-update) | async-done | bytes 32784 | tf_op jit(solution)/shard_map/reduce_scatter | solution.py:241
  248.7 1.9 collective-permute-start.7
  251.3 3.5 collective-permute-done.7
  255.8 2.4 broadcast_in_dim.223
  258.2 2.8 copy.391
  263.7 2.9 fusion.69
  266.7 2.9 fusion.68
  269.6 3.0 fusion.67
  272.6 7.7 %fusion.18 = f32[7,16,64]{2,1,0:T(8,128)S(1)} fusion(bf16[7,64,16,512]{3,2,1,0:T(8,128)(2,1)S(1)} %bitcast.441, bf16[16,16,512]{2,1,0:T(8,128)(2,1)S(1)} %get-tuple-element.11), kind=kOutput, calls=%fused_computation.49 | convolution fusion | flops 117440512 | bytes 7630848 | tf_op jit(solution)/shard_map/blp,bnp->ln/dot_general | solution.py:272
  284.2 1.9 collective-permute-start.8
  286.2 3.6 collective-permute-start.9
  300.2 2.7 fusion.8
  302.9 2.7 fusion.9
  305.6 1.9 fusion.10
  307.5 2.0 fusion.11
  309.6 1.9 fusion.12
  311.5 1.9 fusion.13
  313.4 33.5 %copy.413 = bf16[16,7,16,8,8,8]{2,1,5,4,3,0:T(8,128)(2,1)} copy(bf16[16,7,16,8,8,8]{2,5,4,3,0,1:T(8,128)(2,1)} %bitcast.417) | data formatting | bytes 3670016 | tf_op jit(solution)/shard_map/vmap()/transpose | solution.py:39
  346.9 17.2 %reshape.852 = bf16[16,112,512]{1,2,0:T(8,128)(2,1)S(1)} reshape(bf16[16,7,16,8,8,8]{2,1,5,4,3,0:T(8,128)(2,1)} %copy.413) | data formatting | bytes 3670016 | tf_op jit(solution)/shard_map/vmap()/reshape | solution.py:39
  366.7 170.5 %all-reduce.10.cloned.1.call-done = f32[4,14368]{1,0:T(4,128)} async-done(((f32[4,14368]{1,0:T(4,128)}), f32[4,14368]{1,0:T(4,128)}) %all-reduce.10.cloned.1.call-update) | async-done | bytes 229904 | tf_op jit(solution)/shard_map/psum | solution.py:143
  541.1 22.1 %reduce-scatter.5.cloned.1.call-done = bf16[16,16,512]{2,1,0:T(8,128)(2,1)} async-done(((bf16[16,64,512]{2,1,0:T(8,128)(2,1)}), bf16[16,16,512]{2,1,0:T(8,128)(2,1)}) %reduce-scatter.5.cloned.1.call-update) | async-done | bytes 262160 | tf_op jit(solution)/shard_map/reduce_scatter | solution.py:286
  (284 shorter events, 85.0 us)
Async XLA Ops:
  7.2 32.8 %all-gather.2.cloned.1.call-start = ((), (), s32[]{:S(2)}) async-start(), calls=%async_computation.2 | async-start | bytes 1310720 | tf_op jit(solution)/shard_map/all_gather | solution.py:175
  9.0 238.5 %reduce-scatter.3.cloned.1.call-start = ((), (), s32[]{:S(2)}) async-start(), calls=%async_computation.3 | async-start | bytes 163840 | tf_op jit(solution)/shard_map/reduce_scatter | solution.py:241
  25.6 153.9 %copy-start.26 = (pred[2]{0:T(512)(128)(4,1)}, pred[2]{0:T(512)(128)(4,1)S(1)}, u32[]{:S(2)}) copy-start(pred[2]{0:T(512)(128)(4,1)S(1)} %get-tuple-element.81) | copy-start | bytes 10
  25.6 154.8 %copy-start.25 = (pred[2]{0:T(512)(128)(4,1)}, pred[2]{0:T(512)(128)(4,1)S(1)}, u32[]{:S(2)}) copy-start(pred[2]{0:T(512)(128)(4,1)S(1)} %get-tuple-element.82) | copy-start | bytes 10
  25.6 153.3 %copy-start.24 = (s32[1024]{0:T(1024)}, s32[1024]{0:T(1024)S(1)}, u32[]{:S(2)}) copy-start(s32[1024]{0:T(1024)S(1)} %pad_clamp_fusion.2) | copy-start | bytes 12292
  25.6 154.2 %copy-start.23 = (s32[1024]{0:T(1024)}, s32[1024]{0:T(1024)S(1)}, u32[]{:S(2)}) copy-start(s32[1024]{0:T(1024)S(1)} %pad_clamp_fusion.3) | copy-start | bytes 12292
  53.0 7.2 %collective-permute-start = (bf16[4,3,64,64]{2,3,1,0:T(8,128)(2,1)S(1)}, bf16[4,3,64,64]{2,3,1,0:T(8,128)(2,1)S(1)}, u32[]{:S(2)}, u32[]{:S(2)}) collective-permute-start(bf16[4,3,64,64]{2,3,1,0:T(8,128)(2,1)S(1)} %constant_dynamic-slice_fusion.3), channel_id=1, source_target_pairs={{0,4},{4,8},{8,12},{12,16},{16,20},{20,24},{24,28},{28,32},{32,36}... | collective-permute-start | bytes 294920 | tf_op jit(solution)/shard_map/ppermute | solution.py:13
  54.9 8.7 %collective-permute-start.1 = (bf16[4,3,64,64]{2,3,1,0:T(8,128)(2,1)S(1)}, bf16[4,3,64,64]{2,3,1,0:T(8,128)(2,1)S(1)}, u32[]{:S(2)}, u32[]{:S(2)}) collective-permute-start(bf16[4,3,64,64]{2,3,1,0:T(8,128)(2,1)S(1)} %slice.370), channel_id=1, source_target_pairs={{4,0},{8,4},{12,8},{16,12},{20,16},{24,20},{28,24},{32,28},{36,32}... | collective-permute-start | bytes 294920 | tf_op jit(solution)/shard_map/ppermute | solution.py:13
  69.1 2.2 copy-start.12
  70.3 1.7 copy-start.3
  72.0 2.7 copy-start.2
  74.7 2.7 copy-start.11
  77.4 2.0 copy-start.10
  79.4 1.9 copy-start.9
  81.4 2.0 copy-start.8
  118.9 22.2 %copy-start.27 = (f32[16]{0:T(128)S(1)}, f32[16]{0:T(128)}, u32[]{:S(2)}) copy-start(f32[16]{0:T(128)} %param.13) | copy-start | bytes 196
  151.3 5.0 copy-start.21
  154.3 4.6 collective-permute-start.2
  156.3 31.0 %copy-start.28 = (pred[2]{0:T(512)(128)(4,1)}, pred[2]{0:T(512)(128)(4,1)S(1)}, u32[]{:S(2)}) copy-start(pred[2]{0:T(512)(128)(4,1)S(1)} %iota_compare_fusion.1) | copy-start | bytes 10
  172.8 6.1 %collective-permute-start.4 = (bf16[64,64]{0,1:T(8,128)(2,1)S(1)}, bf16[64,64]{0,1:T(8,128)(2,1)S(1)}, u32[]{:S(2)}, u32[]{:S(2)}) collective-permute-start(bf16[64,64]{0,1:T(8,128)(2,1)S(1)} %slice_bitcast_fusion.31), channel_id=1, source_target_pairs={{4,0},{8,4},{12,8},{16,12},{20,16},{24,20},{28,24},{32,28},{36,32}... | collective-permute-start | bytes 24584 | tf_op jit(solution)/shard_map/ppermute | solution.py:13
  174.7 5.1 collective-permute-start.3
  180.6 1.2 copy-start.15
  186.2 1.1 copy-start.31
  186.2 1.1 copy-start.32
  192.6 11.0 %collective-permute-start.6 = (bf16[16,64]{0,1:T(8,128)(2,1)}, bf16[16,64]{0,1:T(8,128)(2,1)}, u32[]{:S(2)}, u32[]{:S(2)}) collective-permute-start(bf16[16,64]{0,1:T(8,128)(2,1)} %slice_bitcast_fusion.30), channel_id=1, source_target_pairs={{4,0},{8,4},{12,8},{16,12},{20,16},{24,20},{28,24},{32,28},{36,32}... | collective-permute-start | bytes 6152 | tf_op jit(solution)/shard_map/ppermute | solution.py:13
  195.2 8.2 %copy-start.19 = (bf16[2,16,8,7,8]{1,4,3,2,0:T(8,128)(2,1)S(1)}, bf16[2,16,8,7,8]{1,4,3,2,0:T(8,128)(2,1)}, u32[]{:S(2)}) copy-start(bf16[2,16,8,7,8]{1,4,3,2,0:T(8,128)(2,1)} %get-tuple-element.48) | copy-start | bytes 86020
  195.2 10.8 %collective-permute-start.5 = (bf16[16,64]{1,0:T(8,128)(2,1)}, bf16[16,64]{1,0:T(8,128)(2,1)}, u32[]{:S(2)}, u32[]{:S(2)}) collective-permute-start(bf16[16,64]{1,0:T(8,128)(2,1)} %bitcast.86), channel_id=1, source_target_pairs={{0,4},{4,8},{8,12},{12,16},{16,20},{20,24},{24,28},{28,32},{32,36}... | collective-permute-start | bytes 6152 | tf_op jit(solution)/shard_map/ppermute | solution.py:13
  201.1 8.1 %copy-start.18 = (bf16[2,16,7,8,8]{1,4,3,2,0:T(8,128)(2,1)S(1)}, bf16[2,16,7,8,8]{1,4,3,2,0:T(8,128)(2,1)}, u32[]{:S(2)}) copy-start(bf16[2,16,7,8,8]{1,4,3,2,0:T(8,128)(2,1)} %get-tuple-element.44) | copy-start | bytes 86020
  209.3 1.2 copy-start.16
  214.8 2.9 copy-start.22
  217.1 320.1 %all-reduce.10.cloned.1.call-start = ((), (), s32[]{:S(2)}) async-start(), calls=%async_computation.5 | async-start | bytes 462848 | tf_op jit(solution)/shard_map/psum | solution.py:143
  219.5 28.0 %copy-start.29 = (pred[2]{0:T(512)(128)(4,1)S(1)}, pred[2]{0:T(512)(128)(4,1)}, u32[]{:S(2)}) copy-start(pred[2]{0:T(512)(128)(4,1)} %copy-done.28) | copy-start | bytes 10
  248.7 6.1 %collective-permute-start.7 = (bf16[7,16,64]{1,2,0:T(8,128)(2,1)S(1)}, bf16[7,16,64]{1,2,0:T(8,128)(2,1)S(1)}, u32[]{:S(2)}, u32[]{:S(2)}) collective-permute-start(bf16[7,16,64]{1,2,0:T(8,128)(2,1)S(1)} %constant_dynamic-slice_fusion.1), channel_id=1, source_target_pairs={{0,4},{4,8},{8,12},{12,16},{16,20},{20,24},{24,28},{28,32},{32,36}... | collective-permute-start | bytes 43016 | tf_op jit(solution)/shard_map/ppermute | solution.py:13
  258.2 2.9 copy-start.14
  263.7 8.9 %slice-start = ((s8[7340032]{0:T(1024)(128)(4,1)}), s8[4194304]{0:T(1024)(128)(4,1)S(1)}, s32[]{:S(2)}) async-start(s8[7340032]{0:T(1024)(128)(4,1)} %bitcast.439), calls=%async_computation.6 | async-start | bytes 8388608
  266.7 5.9 %slice-start.1 = ((s8[7340032]{0:T(1024)(128)(4,1)}), s8[3145728]{0:T(1024)(128)(4,1)S(1)}, s32[]{:S(2)}) async-start(s8[7340032]{0:T(1024)(128)(4,1)} %bitcast.439), calls=%async_computation.7 | async-start | bytes 6291456
  272.6 7.8 %copy-start.30 = (f32[16]{0:T(128)S(1)}, f32[16]{0:T(128)}, u32[]{:S(2)}) copy-start(f32[16]{0:T(128)} %get-tuple-element.8) | copy-start | bytes 196
  282.6 280.6 %reduce-scatter.5.cloned.1.call-start = ((), (), s32[]{:S(2)}) async-start(), calls=%async_computation.4 | async-start | bytes 1310720 | tf_op jit(solution)/shard_map/reduce_scatter | solution.py:286
  283.3 0.9 copy-start.13
  284.2 9.0 %collective-permute-start.8 = (bf16[4,3,16,64]{2,3,1,0:T(8,128)(2,1)S(1)}, bf16[4,3,16,64]{2,3,1,0:T(8,128)(2,1)}, u32[]{:S(2)}, u32[]{:S(2)}) collective-permute-start(bf16[4,3,16,64]{2,3,1,0:T(8,128)(2,1)S(1)} %constant_dynamic-slice_fusion), channel_id=1, source_target_pairs={{0,4},{4,8},{8,12},{12,16},{16,20},{20,24},{24,28},{28,32},{32,36}... | collective-permute-start | bytes 73736 | tf_op jit(solution)/shard_map/ppermute | solution.py:13
  286.2 9.1 %collective-permute-start.9 = (bf16[4,3,16,64]{2,3,1,0:T(8,128)(2,1)S(1)}, bf16[4,3,16,64]{2,3,1,0:T(8,128)(2,1)S(1)}, u32[]{:S(2)}, u32[]{:S(2)}) collective-permute-start(bf16[4,3,16,64]{2,3,1,0:T(8,128)(2,1)S(1)} %slice.420), channel_id=1, source_target_pairs={{4,0},{8,4},{12,8},{16,12},{20,16},{24,20},{28,24},{32,28},{36,32}... | collective-permute-start | bytes 73736 | tf_op jit(solution)/shard_map/ppermute | solution.py:13
  298.6 1.6 copy-start.1
  300.2 2.7 copy-start
  302.9 2.7 copy-start.7
  305.6 1.9 copy-start.6
  307.5 2.0 copy-start.5
  309.6 1.9 copy-start.4
  346.9 17.2 %copy-start.20 = (bf16[7,16,64]{2,1,0:T(8,128)(2,1)S(1)}, bf16[7,16,64]{2,1,0:T(8,128)(2,1)}, u32[]{:S(2)}) copy-start(bf16[7,16,64]{2,1,0:T(8,128)(2,1)} %gather_fusion.11) | copy-start | bytes 43012
  (1 other events, 0.7 us)
Sparse Core Ops, SparseCore 0:
  10.4 29.5 all-gather.1
  217.2 30.2 reduce-scatter.2
  282.7 254.4 all-reduce.9
  539.6 23.5 reduce-scatter.4
where the time goes:
time: 580 us; the launch traced here: 572 us
  waiting for transfers between devices  224 us (39%)
  local copies, waits for them, and re-layouts  217 us (37%)
  other arithmetic  48.9 us (8%)
  starting transfers between devices  28.5 us (5%)
  between operations  21.9 us (4%)
  matrix products  19.2 us (3%)
  blocking collectives  12 us (2%)
    psum x1, waiting for transfers between devices, sum_over_blocks(): summed = lax.psum(slots, ('blocks', 'chan'))  170 us
    transpose x4, local copies, waits for them, and re-layouts, block_views(): return stacked.reshape(7 * channels, edge_cells ** 3)  75.6 us
    reshape x4, local copies, waits for them, and re-layouts, block_views(): return stacked.reshape(7 * channels, edge_cells ** 3)  41.7 us
    ppermute x10, starting transfers between devices, from_behind(): return lax.ppermute(block, axis, route)  28.4 us
    unnamed x13, other arithmetic  23.8 us
    reduce_scatter x1, waiting for transfers between devices, local(): lax.psum_scatter(fine_partial.astype(jnp.bfloat16), 'chan', scatter_dimen...  22.1 us
    dot_general x1, local copies, waits for them, and re-layouts, local(): jnp.einsum('blp,bnp->ln', fine_delta, fine_views, preferred_element_type=...  14.8 us
    unnamed x103, local copies, waits for them, and re-layouts  13.7 us
  transfers between devices with their start and end apart: 14, of which 7 were waited for; matrix products, arithmetic and copies ran while one was open for 21% of the time, Pallas kernels for 0%

commit v1 on v0

--- a/solution.py
+++ b/solution.py
@@ -172,7 +172,9 @@
     coarse_ids = coarse_first + jnp.arange(coarse_slots, dtype=jnp.int32)
     live_mask = (jnp.arange(slot_count) < live_count)[:, None, None]
     coarse_live = (jnp.arange(coarse_slots) < coarse_count)[:, None, None]
-    full_input = lax.all_gather(fine_input, "chan", axis=1, tiled=True)
+    full_input = jnp.concatenate(
+        lax.all_to_all(jnp.stack([fine_input] * lax.axis_size("chan")), "chan", 0, 0), axis=1
+    )
     fine_cubes = full_input.reshape(slot_count, channels, EDGE, EDGE, EDGE)
     input_halos = fine_halo(
         jax.vmap(block_layers)(fine_cubes), block_ids, first_block, live_count, total_blocks

time: 580 us -> 601 us (1.036)
  local copies, waits for them, and re-layouts: 217 us -> 242 us
  waiting for transfers between devices: 224 us -> 214 us
  starting transfers between devices: 28.5 us -> 34.9 us
    another operation x1 -> x4, local copies, waits for them, and re-layouts: 0.74 us -> 22.3 us  [the longest x1 10.5 us: block_views(): jnp.stack([block_cube, minus_x, plus_x, minus_y, plus_y, minus_z, plus_z])]
    all_gather x1 -> x0, waiting for transfers between devices: 13.6 us -> none  [local(): full_input = lax.all_gather(fine_input, 'chan', axis=1, tiled=True)]
    reshape x0 -> x1, local copies, waits for them, and re-layouts: none -> 8.94 us  [local(): jnp.concatenate(lax.all_to_all(jnp.stack([fine_input] * lax.axis_size('ch...]
    unnamed x103 -> x114, local copies, waits for them, and re-layouts: 13.7 us -> 11.9 us
  transfers between devices with their start and end apart: 14 -> 14, of which waited for: 7 -> 8; matrix products, arithmetic and copies ran while one was open for 21% -> 20% of each run, Pallas kernels for 0% -> 0%
where the time goes in v1:
time: 601 us; the launch traced here: 591 us
  local copies, waits for them, and re-layouts  242 us (40%)
  waiting for transfers between devices  214 us (36%)
  other arithmetic  46.8 us (8%)
  starting transfers between devices  34.9 us (6%)
  between operations  22.2 us (4%)
  matrix products  19.2 us (3%)
  blocking collectives  12 us (2%)
    psum x1, waiting for transfers between devices, sum_over_blocks(): summed = lax.psum(slots, ('blocks', 'chan'))  170 us
    transpose x4, local copies, waits for them, and re-layouts, block_views(): return stacked.reshape(7 * channels, edge_cells ** 3)  75.6 us
    reshape x4, local copies, waits for them, and re-layouts, block_views(): return stacked.reshape(7 * channels, edge_cells ** 3)  41.8 us
    ppermute x10, starting transfers between devices, from_behind(): return lax.ppermute(block, axis, route)  30.4 us
    unnamed x13, other arithmetic  23.8 us
    reduce_scatter x1, waiting for transfers between devices, local(): lax.psum_scatter(fine_partial.astype(jnp.bfloat16), 'chan', scatter_dimen...  22.3 us
    dot_general x1, local copies, waits for them, and re-layouts, local(): jnp.einsum('blp,bnp->ln', fine_delta, fine_views, preferred_element_type=...  14.8 us
    reduce_scatter x1, waiting for transfers between devices, local(): lax.psum_scatter(partial_sums.astype(jnp.bfloat16), 'chan', scatter_dimen...  14 us
  transfers between devices with their start and end apart: 14, of which 8 were waited for; matrix products, arithmetic and copies ran while one was open for 20% of the time, Pallas kernels for 0%

profile of v1, /device:TPU:6, one launch (start us, length us, event | category | flops | bytes accessed | tf_op | source)
XLA Modules:
  0.0 591.3 jit_solution(3378192622714761717)
XLA Ops:
  7.2 2.1 stack.141
  9.4 4.5 all-to-all-start
  28.9 8.9 %copy.322 = bf16[16,4,16,512]{2,1,3,0:T(4,128)(2,1)} copy(bf16[16,4,16,512]{3,2,0,1:T(8,128)(2,1)S(1)} %bitcast.438) | data formatting | bytes 2097152 | tf_op jit(solution)/shard_map/reshape | solution.py:175
  37.9 9.5 %reshape_reshape.9 = bf16[16,64,8,8,8]{1,4,3,2,0:T(8,128)(2,1)S(1)} reshape(bf16[16,4,16,512]{2,1,3,0:T(4,128)(2,1)} %copy.322) | data formatting | bytes 2097152 | tf_op jit(solution)/shard_map/reshape;reshape | solution.py:178
  48.5 3.0 fusion.73
  51.5 10.5 %stack_reshape_reshape.3 = bf16[1,16,64,8,8,8]{2,5,4,3,1,0:T(8,128)(2,1)} reshape(bf16[16,4,16,512]{2,1,3,0:T(4,128)(2,1)} %copy.322) | data formatting | bytes 2097152 | tf_op jit(solution)/shard_map/vmap()/stack;reshape;reshape | solution.py:38
  62.0 2.9 fusion.72
  64.9 3.0 fusion.71
  68.6 2.1 collective-permute-start
  70.7 3.6 collective-permute-start.1
  87.9 2.7 fusion.2
  90.6 2.7 fusion.3
  93.3 2.0 fusion.4
  95.3 1.9 fusion.5
  97.2 2.0 fusion.6
  99.3 1.9 fusion.7
  101.2 33.5 %copy.341 = bf16[16,7,64,8,8,8]{2,1,5,4,3,0:T(8,128)(2,1)} copy(bf16[16,7,64,8,8,8]{2,5,4,3,0,1:T(8,128)(2,1)} %bitcast.412) | data formatting | bytes 14680064 | tf_op jit(solution)/shard_map/vmap()/transpose | solution.py:39
  134.7 22.2 %reshape.838 = bf16[16,448,512]{1,2,0:T(8,128)(2,1)} reshape(bf16[16,7,64,8,8,8]{2,1,5,4,3,0:T(8,128)(2,1)} %copy.341) | data formatting | bytes 14680064 | tf_op jit(solution)/shard_map/vmap()/reshape | solution.py:39
  156.9 6.5 %fusion.21 = (f32[16,16,512]{2,1,0:T(8,128)S(1)}, f32[16,16,512]{2,1,0:T(8,128)}) fusion(f32[16]{0:T(128)S(1)} %copy-done.29, bf16[16,448,512]{1,2,0:T(8,128)(2,1)} %reshape.838, bf16[16,448,1]{1,0,2:T(8,128)(2,1)S(1)} %reshape.953), kind=kOutput, calls=%fused_computation.62 | convolution fusion | flops 118358016 | bytes 8403008 | tf_op jit(solution)/shard_map/ln,bnp->blp/dot_general | solution.py:185
  163.4 3.7 copy.344
  167.1 2.8 reduce_sum.37
  170.1 3.8 collective-permute-start.2
  174.9 2.0 collective-permute-done.2
  178.0 12.0 %all_gather.3 = bf16[2,64,512]{2,1,0:T(8,128)(2,1)S(1)} all-gather(bf16[2,16,512]{2,1,0:T(8,128)(2,1)S(1)} %broadcast_select_fusion.4), channel_id=1, replica_groups=mesh['blocks'=64,'chan'=4] {'chan'}, dimensions={1}, use_global_device_ids=true | all-gather | bytes 163840 | tf_op jit(solution)/shard_map/all_gather | solution.py:204
  190.7 1.9 collective-permute-start.4
  192.7 3.7 collective-permute-start.3
  199.8 4.3 copy.361
  213.1 5.9 collective-permute-start.5
  228.4 4.3 copy.380
  237.5 14.8 %copy.413 = bf16[448,16,512]{2,1,0:T(8,128)(2,1)} copy(bf16[448,16,512]{0,2,1:T(8,128)(2,1)} %bitcast.410) | data formatting | bytes 14680064 | tf_op jit(solution)/shard_map/blp,bnp->ln/dot_general | solution.py:274
  252.8 14.0 %reduce-scatter.3.cloned.1.call-done = bf16[2,16,512]{2,1,0:T(8,128)(2,1)} async-done(((bf16[2,64,512]{2,1,0:T(8,128)(2,1)}), bf16[2,16,512]{2,1,0:T(8,128)(2,1)}) %reduce-scatter.3.cloned.1.call-update) | async-done | bytes 32784 | tf_op jit(solution)/shard_map/reduce_scatter | solution.py:243
  267.9 1.9 collective-permute-start.7
  270.5 3.5 collective-permute-done.7
  275.0 2.4 broadcast_in_dim.223
  277.4 2.8 copy.388
  282.9 3.0 fusion.69
  285.9 2.9 fusion.68
  288.8 3.0 fusion.67
  291.9 7.7 %fusion.18 = f32[7,16,64]{2,1,0:T(8,128)S(1)} fusion(bf16[7,64,16,512]{3,2,1,0:T(8,128)(2,1)S(1)} %bitcast.435, bf16[16,16,512]{2,1,0:T(8,128)(2,1)S(1)} %get-tuple-element.11), kind=kOutput, calls=%fused_computation.49 | convolution fusion | flops 117440512 | bytes 7630848 | tf_op jit(solution)/shard_map/blp,bnp->ln/dot_general | solution.py:274
  303.5 1.9 collective-permute-start.8
  305.4 3.6 collective-permute-start.9
  319.4 2.7 fusion.8
  322.1 2.7 fusion.9
  326.8 2.0 fusion.11
  332.7 33.5 %copy.410 = bf16[16,7,16,8,8,8]{2,1,5,4,3,0:T(8,128)(2,1)} copy(bf16[16,7,16,8,8,8]{2,5,4,3,0,1:T(8,128)(2,1)} %bitcast.411) | data formatting | bytes 3670016 | tf_op jit(solution)/shard_map/vmap()/transpose | solution.py:39
  366.2 17.2 %reshape.854 = bf16[16,112,512]{1,2,0:T(8,128)(2,1)S(1)} reshape(bf16[16,7,16,8,8,8]{2,1,5,4,3,0:T(8,128)(2,1)} %copy.410) | data formatting | bytes 3670016 | tf_op jit(solution)/shard_map/vmap()/reshape | solution.py:39
  386.0 170.4 %all-reduce.10.cloned.1.call-done = f32[4,14368]{1,0:T(4,128)} async-done(((f32[4,14368]{1,0:T(4,128)}), f32[4,14368]{1,0:T(4,128)}) %all-reduce.10.cloned.1.call-update) | async-done | bytes 229904 | tf_op jit(solution)/shard_map/psum | solution.py:143
  560.2 22.3 %reduce-scatter.5.cloned.1.call-done = bf16[16,16,512]{2,1,0:T(8,128)(2,1)} async-done(((bf16[16,64,512]{2,1,0:T(8,128)(2,1)}), bf16[16,16,512]{2,1,0:T(8,128)(2,1)}) %reduce-scatter.5.cloned.1.call-update) | async-done | bytes 262160 | tf_op jit(solution)/shard_map/reduce_scatter | solution.py:288
  (297 shorter events, 86.6 us)
Async XLA Ops:
  7.2 17.4 %copy-start.35 = (s32[3]{0:T(128)S(1)}, s32[3]{0:T(128)}, u32[]{:S(2)}) copy-start(s32[3]{0:T(128)} %constant.184.clone) | copy-start | bytes 40
  7.2 17.4 %copy-start.36 = (s32[3]{0:T(128)S(1)}, s32[3]{0:T(128)}, u32[]{:S(2)}) copy-start(s32[3]{0:T(128)} %constant.203) | copy-start | bytes 40
  7.2 20.1 %copy-start.34 = (s32[7]{0:T(128)S(1)}, s32[7]{0:T(128)}, u32[]{:S(2)}) copy-start(s32[7]{0:T(128)} %constant.260) | copy-start | bytes 88
  7.2 6.6 %copy-start.32 = (s32[64]{0:T(128)S(1)}, s32[64]{0:T(128)}, u32[]{:S(2)}) copy-start(s32[64]{0:T(128)} %param.11) | copy-start | bytes 772
  7.2 19.8 %copy-start.23 = (bf16[7,16,64]{2,1,0:T(8,128)(2,1)S(1)}, bf16[7,16,64]{2,1,0:T(8,128)(2,1)}, u32[]{:S(2)}) copy-start(bf16[7,16,64]{2,1,0:T(8,128)(2,1)} %param.12) | copy-start | bytes 43012
  9.4 19.6 %all-to-all-start = ((bf16[4,16,16,512]{3,2,1,0:T(8,128)(2,1)}), bf16[4,16,16,512]{3,2,1,0:T(8,128)(2,1)S(1)}, u32[]{:S(2)}, u32[]{:S(2)}) async-start(bf16[4,16,16,512]{3,2,1,0:T(8,128)(2,1)} %stack.141), calls=%async_computation | async-start | bytes 2097152 | tf_op jit(solution)/shard_map/all_to_all | solution.py:176
  13.8 252.9 %reduce-scatter.3.cloned.1.call-start = ((), (), s32[]{:S(2)}) async-start(), calls=%async_computation.3 | async-start | bytes 163840 | tf_op jit(solution)/shard_map/reduce_scatter | solution.py:243
  27.2 170.2 %copy-start.28 = (pred[2]{0:T(512)(128)(4,1)}, pred[2]{0:T(512)(128)(4,1)S(1)}, u32[]{:S(2)}) copy-start(pred[2]{0:T(512)(128)(4,1)S(1)} %get-tuple-element.81) | copy-start | bytes 10
  27.3 171.1 %copy-start.27 = (pred[2]{0:T(512)(128)(4,1)}, pred[2]{0:T(512)(128)(4,1)S(1)}, u32[]{:S(2)}) copy-start(pred[2]{0:T(512)(128)(4,1)S(1)} %get-tuple-element.82) | copy-start | bytes 10
  27.3 169.6 %copy-start.26 = (s32[1024]{0:T(1024)}, s32[1024]{0:T(1024)S(1)}, u32[]{:S(2)}) copy-start(s32[1024]{0:T(1024)S(1)} %pad_clamp_fusion.2) | copy-start | bytes 12292
  27.3 170.4 %copy-start.25 = (s32[1024]{0:T(1024)}, s32[1024]{0:T(1024)S(1)}, u32[]{:S(2)}) copy-start(s32[1024]{0:T(1024)S(1)} %pad_clamp_fusion.3) | copy-start | bytes 12292
  68.4 5.9 %copy-start = (bf16[1,16,64,8,8,8]{2,5,4,3,1,0:T(8,128)(2,1)S(1)}, bf16[1,16,64,8,8,8]{2,5,4,3,1,0:T(8,128)(2,1)}, u32[]{:S(2)}) copy-start(bf16[1,16,64,8,8,8]{2,5,4,3,1,0:T(8,128)(2,1)} %stack_reshape_reshape.3) | copy-start | bytes 3145732
  68.6 7.2 %collective-permute-start = (bf16[4,3,64,64]{2,3,1,0:T(8,128)(2,1)S(1)}, bf16[4,3,64,64]{2,3,1,0:T(8,128)(2,1)S(1)}, u32[]{:S(2)}, u32[]{:S(2)}) collective-permute-start(bf16[4,3,64,64]{2,3,1,0:T(8,128)(2,1)S(1)} %constant_dynamic-slice_fusion.3), channel_id=1, source_target_pairs={{0,4},{4,8},{8,12},{12,16},{16,20},{20,24},{24,28},{28,32},{32,36}... | collective-permute-start | bytes 294920 | tf_op jit(solution)/shard_map/ppermute | solution.py:13
  70.7 6.8 %collective-permute-start.1 = (bf16[4,3,64,64]{2,3,1,0:T(8,128)(2,1)S(1)}, bf16[4,3,64,64]{2,3,1,0:T(8,128)(2,1)S(1)}, u32[]{:S(2)}, u32[]{:S(2)}) collective-permute-start(bf16[4,3,64,64]{2,3,1,0:T(8,128)(2,1)S(1)} %slice.370), channel_id=1, source_target_pairs={{4,0},{8,4},{12,8},{16,12},{20,16},{24,20},{28,24},{32,28},{36,32}... | collective-permute-start | bytes 294920 | tf_op jit(solution)/shard_map/ppermute | solution.py:13
  85.0 2.2 copy-start.13
  86.2 1.7 copy-start.4
  87.9 2.7 copy-start.3
  90.6 2.7 copy-start.12
  93.3 2.0 copy-start.11
  95.3 1.9 copy-start.10
  97.2 2.0 copy-start.9
  134.7 22.3 %copy-start.29 = (f32[16]{0:T(128)S(1)}, f32[16]{0:T(128)}, u32[]{:S(2)}) copy-start(f32[16]{0:T(128)} %param.13) | copy-start | bytes 196
  167.1 6.8 %copy-start.22 = (bf16[7,16,64]{2,1,0:T(8,128)(2,1)S(1)}, bf16[7,16,64]{2,1,0:T(8,128)(2,1)}, u32[]{:S(2)}) copy-start(bf16[7,16,64]{2,1,0:T(8,128)(2,1)} %param.14) | copy-start | bytes 43012
  170.1 6.8 %collective-permute-start.2 = (bf16[7,16,64]{2,1,0:T(8,128)(2,1)S(1)}, bf16[7,16,64]{2,1,0:T(8,128)(2,1)S(1)}, u32[]{:S(2)}, u32[]{:S(2)}) collective-permute-start(bf16[7,16,64]{2,1,0:T(8,128)(2,1)S(1)} %copy.346), channel_id=1, source_target_pairs={{4,0},{8,4},{12,8},{16,12},{20,16},{24,20},{28,24},{32,28},{36,32}... | collective-permute-start | bytes 43016 | tf_op jit(solution)/shard_map/ppermute | solution.py:13
  173.9 31.3 %copy-start.30 = (pred[2]{0:T(512)(128)(4,1)}, pred[2]{0:T(512)(128)(4,1)S(1)}, u32[]{:S(2)}) copy-start(pred[2]{0:T(512)(128)(4,1)S(1)} %iota_compare_fusion.1) | copy-start | bytes 10
  190.7 6.1 %collective-permute-start.4 = (bf16[64,64]{0,1:T(8,128)(2,1)S(1)}, bf16[64,64]{0,1:T(8,128)(2,1)S(1)}, u32[]{:S(2)}, u32[]{:S(2)}) collective-permute-start(bf16[64,64]{0,1:T(8,128)(2,1)S(1)} %slice_bitcast_fusion.31), channel_id=1, source_target_pairs={{4,0},{8,4},{12,8},{16,12},{20,16},{24,20},{28,24},{32,28},{36,32}... | collective-permute-start | bytes 24584 | tf_op jit(solution)/shard_map/ppermute | solution.py:13
  192.7 5.1 collective-permute-start.3
  210.5 11.0 %collective-permute-start.6 = (bf16[16,64]{0,1:T(8,128)(2,1)}, bf16[16,64]{0,1:T(8,128)(2,1)}, u32[]{:S(2)}, u32[]{:S(2)}) collective-permute-start(bf16[16,64]{0,1:T(8,128)(2,1)} %slice_bitcast_fusion.30), channel_id=1, source_target_pairs={{4,0},{8,4},{12,8},{16,12},{20,16},{24,20},{28,24},{32,28},{36,32}... | collective-permute-start | bytes 6152 | tf_op jit(solution)/shard_map/ppermute | solution.py:13
  213.1 8.2 %copy-start.20 = (bf16[2,16,8,7,8]{1,4,3,2,0:T(8,128)(2,1)S(1)}, bf16[2,16,8,7,8]{1,4,3,2,0:T(8,128)(2,1)}, u32[]{:S(2)}) copy-start(bf16[2,16,8,7,8]{1,4,3,2,0:T(8,128)(2,1)} %get-tuple-element.48) | copy-start | bytes 86020
  213.1 10.8 %collective-permute-start.5 = (bf16[16,64]{1,0:T(8,128)(2,1)}, bf16[16,64]{1,0:T(8,128)(2,1)}, u32[]{:S(2)}, u32[]{:S(2)}) collective-permute-start(bf16[16,64]{1,0:T(8,128)(2,1)} %bitcast.85), channel_id=1, source_target_pairs={{0,4},{4,8},{8,12},{12,16},{16,20},{20,24},{24,28},{28,32},{32,36}... | collective-permute-start | bytes 6152 | tf_op jit(solution)/shard_map/ppermute | solution.py:13
  219.0 8.0 %copy-start.19 = (bf16[2,16,7,8,8]{1,4,3,2,0:T(8,128)(2,1)S(1)}, bf16[2,16,7,8,8]{1,4,3,2,0:T(8,128)(2,1)}, u32[]{:S(2)}) copy-start(bf16[2,16,7,8,8]{1,4,3,2,0:T(8,128)(2,1)} %get-tuple-element.44) | copy-start | bytes 86020
  232.7 2.9 copy-start.24
  234.9 321.4 %all-reduce.10.cloned.1.call-start = ((), (), s32[]{:S(2)}) async-start(), calls=%async_computation.5 | async-start | bytes 462848 | tf_op jit(solution)/shard_map/psum | solution.py:143
  237.5 29.2 %copy-start.31 = (pred[2]{0:T(512)(128)(4,1)S(1)}, pred[2]{0:T(512)(128)(4,1)}, u32[]{:S(2)}) copy-start(pred[2]{0:T(512)(128)(4,1)} %copy-done.30) | copy-start | bytes 10
  267.9 6.1 %collective-permute-start.7 = (bf16[7,16,64]{1,2,0:T(8,128)(2,1)S(1)}, bf16[7,16,64]{1,2,0:T(8,128)(2,1)S(1)}, u32[]{:S(2)}, u32[]{:S(2)}) collective-permute-start(bf16[7,16,64]{1,2,0:T(8,128)(2,1)S(1)} %constant_dynamic-slice_fusion.1), channel_id=1, source_target_pairs={{0,4},{4,8},{8,12},{12,16},{16,20},{20,24},{24,28},{28,32},{32,36}... | collective-permute-start | bytes 43016 | tf_op jit(solution)/shard_map/ppermute | solution.py:13
  277.4 2.9 copy-start.15
  282.9 8.9 %slice-start = ((s8[7340032]{0:T(1024)(128)(4,1)}), s8[4194304]{0:T(1024)(128)(4,1)S(1)}, s32[]{:S(2)}) async-start(s8[7340032]{0:T(1024)(128)(4,1)} %bitcast.433), calls=%async_computation.6 | async-start | bytes 8388608
  285.9 6.0 %slice-start.1 = ((s8[7340032]{0:T(1024)(128)(4,1)}), s8[3145728]{0:T(1024)(128)(4,1)S(1)}, s32[]{:S(2)}) async-start(s8[7340032]{0:T(1024)(128)(4,1)} %bitcast.433), calls=%async_computation.7 | async-start | bytes 6291456
  291.8 7.8 %copy-start.33 = (f32[16]{0:T(128)S(1)}, f32[16]{0:T(128)}, u32[]{:S(2)}) copy-start(f32[16]{0:T(128)} %get-tuple-element.8) | copy-start | bytes 196
  301.8 280.7 %reduce-scatter.5.cloned.1.call-start = ((), (), s32[]{:S(2)}) async-start(), calls=%async_computation.4 | async-start | bytes 1310720 | tf_op jit(solution)/shard_map/reduce_scatter | solution.py:288
  303.5 8.9 %collective-permute-start.8 = (bf16[4,3,16,64]{2,3,1,0:T(8,128)(2,1)S(1)}, bf16[4,3,16,64]{2,3,1,0:T(8,128)(2,1)}, u32[]{:S(2)}, u32[]{:S(2)}) collective-permute-start(bf16[4,3,16,64]{2,3,1,0:T(8,128)(2,1)S(1)} %constant_dynamic-slice_fusion), channel_id=1, source_target_pairs={{0,4},{4,8},{8,12},{12,16},{16,20},{20,24},{24,28},{28,32},{32,36}... | collective-permute-start | bytes 73736 | tf_op jit(solution)/shard_map/ppermute | solution.py:13
  305.4 9.1 %collective-permute-start.9 = (bf16[4,3,16,64]{2,3,1,0:T(8,128)(2,1)S(1)}, bf16[4,3,16,64]{2,3,1,0:T(8,128)(2,1)S(1)}, u32[]{:S(2)}, u32[]{:S(2)}) collective-permute-start(bf16[4,3,16,64]{2,3,1,0:T(8,128)(2,1)S(1)} %slice.420), channel_id=1, source_target_pairs={{4,0},{8,4},{12,8},{16,12},{20,16},{24,20},{28,24},{32,28},{36,32}... | collective-permute-start | bytes 73736 | tf_op jit(solution)/shard_map/ppermute | solution.py:13
  319.4 2.7 copy-start.1
  322.1 2.7 copy-start.8
  324.9 1.9 copy-start.7
  326.8 2.0 copy-start.6
  328.8 1.9 copy-start.5
  366.2 17.2 %copy-start.21 = (bf16[7,16,64]{2,1,0:T(8,128)(2,1)S(1)}, bf16[7,16,64]{2,1,0:T(8,128)(2,1)}, u32[]{:S(2)}) copy-start(bf16[7,16,64]{2,1,0:T(8,128)(2,1)} %gather_fusion.11) | copy-start | bytes 43012
  (7 other events, 7.9 us)
Sparse Core Ops, SparseCore 0:
  235.1 31.6 reduce-scatter.2
  301.9 254.3 all-reduce.9
  558.9 23.5 reduce-scatter.4
